TPU v7x, 256 devices: a whole 4x4x8 slice. The times are simulated.
256 devices in a mesh: depth: 16 (over y, z_hi), chan: 16 (over x, z_lo, core).
Axes of the slice: x: 4, y: 4, z: 8 (z_hi: 4, z_lo: 2; z = z_hi * 2 + z_lo), core: 2. Of those that a mesh axis runs over, the one named last changes fastest.
Arguments:
- volume: bfloat16 [256, 16, 4096], P('chan', 'depth'), may hold values from -6 to 6
- w_first: bfloat16 [27, 256, 256], P(None, 'chan'), may hold values from -0.078125 to 0.078125
- b_first: float32 [256], P('chan'), may hold values from -3 to 3
- w_second: bfloat16 [27, 256, 256], P(None, None, 'chan'), may hold values from -0.078125 to 0.078125
- b_second: float32 [256], P('chan'), may hold values from -3 to 3
Outputs:
- block_out: bfloat16 [256, 16, 4096], P('chan', 'depth')
All inputs are finite; a program needn't handle non-finite values.
Results may differ from a plain program's by a relative error of at most 0.0043.
Values may be sent and summed in bfloat16 or wider, within the bound.
No kernel may reach another device: no remote copies, remote signals or barrier semaphores. Data moves between devices by JAX's collectives and lax.ppermute only.
A program may use at most 128 MiB of HBM per device.

v0:
```python
import jax
import jax.numpy as jnp
from jax import lax
from jax.sharding import PartitionSpec as P

W = 64


def extended(array, sides, width):
    for axis, dim in sides:
        peers, length = (lax.axis_size(axis), array.shape[dim])
        up = [(i, (i + 1) % peers) for i in range(peers - 1)]
        down = [(j, i) for i, j in up]
        last = lax.slice_in_dim(array, length - width, length, axis=dim)
        leading = lax.slice_in_dim(array, 0, width, axis=dim)
        before = lax.ppermute(last, axis, up)
        after = lax.ppermute(leading, axis, down)
        array = jnp.concatenate([before, array, after], axis=dim)
    return array


def pad_cells(source):
    return jnp.pad(source, ((0, 0), (0, 0), (W + 1, W + 1)))


def nine_taps(segment):
    seg_chan, planes, cell_count = segment.shape
    padded = pad_cells(segment)
    column = jnp.arange(cell_count) % W
    left_ok = column >= 1
    right_ok = column < W - 1
    per_plane = []
    for plane in range(planes):
        windows = []
        for row_tap in range(3):
            for col_tap in range(3):
                begin = row_tap * W + col_tap
                window = padded[:, plane, begin : begin + cell_count]
                if col_tap == 0:
                    window = jnp.where(left_ok, window, jnp.zeros_like(window))
                elif col_tap == 2:
                    window = jnp.where(right_ok, window, jnp.zeros_like(window))
                windows.append(window)
        per_plane.append(jnp.concatenate(windows, 0))
    return jnp.concatenate(per_plane, 1)


def fold_planes(filters, running, segment):
    seg_chan, padded_depth, cell_count = segment.shape
    slab_depth = padded_depth - 2
    out_chan = filters.shape[2]
    grouped = filters.reshape(3, 9 * seg_chan, out_chan)
    columns = nine_taps(segment)
    total = running
    for depth_tap in range(3):
        window = columns[:, depth_tap * cell_count : (depth_tap + slab_depth) * cell_count]
        total = total + lax.dot_general(
            grouped[depth_tap], window, (((0,), (0,)), ((), ())), preferred_element_type=jnp.float32
        )
    return total


def tap_columns(rimmed):
    chan_local, padded_depth, cell_count = rimmed.shape
    padded = pad_cells(rimmed)
    column = jnp.arange(cell_count) % W
    left_ok = column >= 1
    right_ok = column < W - 1
    gathered_taps = []
    for depth_tap in range(3):
        for row_tap in range(3):
            for col_tap in range(3):
                begin = row_tap * W + col_tap
                window = padded[:, depth_tap, begin : begin + cell_count]
                if col_tap == 0:
                    window = jnp.where(left_ok, window, jnp.zeros_like(window))
                elif col_tap == 2:
                    window = jnp.where(right_ok, window, jnp.zeros_like(window))
                gathered_taps.append(window)
    per_plane = [jnp.concatenate(gathered_taps, 0)]
    return per_plane


def body(volume, w_first, b_first, w_second, b_second):
    chan_local, slab_depth, cell_count = volume.shape
    rimmed = extended(volume, (("depth", 1),), 1)
    empty_sum = jnp.zeros((chan_local, slab_depth * cell_count), jnp.float32)
    per_plane = tap_columns(rimmed)
    flat_filters = w_first.reshape(27 * chan_local, w_first.shape[2])
    pieces = [
        lax.dot_general(
            flat_filters, plane_cols, (((0,), (0,)), ((), ())), preferred_element_type=jnp.float32
        )
        for plane_cols in per_plane
    ]
    first_sum = lax.psum_scatter(
        jnp.stack(pieces, 1).reshape(chan_local * lax.axis_size("chan"), slab_depth * cell_count),
        "chan",
        scatter_dimension=0,
        tiled=True,
    )
    hidden = jnp.maximum(first_sum + b_first[:, None], 0.0).astype(jnp.bfloat16)
    hidden = hidden.reshape(chan_local, slab_depth, cell_count)
    hidden_rim = extended(hidden, (("depth", 1),), 1)
    second_sum = fold_planes(
        w_second, empty_sum, lax.all_gather(hidden_rim, "chan", axis=0, tiled=True)
    )
    block_out = (second_sum + b_second[:, None]).astype(jnp.bfloat16)
    return block_out.reshape(chan_local, slab_depth, cell_count)


def solution(mesh):
    in_specs = (
        P("chan", "depth", None),
        P(None, "chan", None),
        P("chan"),
        P(None, None, "chan"),
        P("chan"),
    )
    out_specs = P("chan", "depth", None)
    return jax.shard_map(body, mesh=mesh, in_specs=in_specs, out_specs=out_specs, check_vma=False)
```

profile of v0, /device:TPU:1, one launch (start us, length us, event | category | flops | bytes accessed | tf_op | source)
XLA Modules:
  0.0 243.7 jit_solution(11958815443732724612)
XLA Ops:
  6.5 5.8 %collective-permute-start = (bf16[16,1,4096]{2,0,1:T(8,128)(2,1)}, bf16[16,1,4096]{2,0,1:T(8,128)(2,1)S(1)}, u32[]{:S(2)}, u32[]{:S(2)}) collective-permute-start(bf16[16,1,4096]{2,0,1:T(8,128)(2,1)} %param.5), channel_id=1, source_target_pairs={{0,16},{16,32},{32,48},{48,64},{64,80},{80,96},{96,112},{112,128},... | collective-permute-start | bytes 393224 | tf_op jit(solution)/shard_map/ppermute | solution.py:16
  12.4 1.3 collective-permute-start.1
  13.7 1.1 collective-permute-done
  14.9 10.2 %collective-permute-done.1 = bf16[16,1,4096]{2,0,1:T(8,128)(2,1)S(1)} collective-permute-done((bf16[16,1,4096]{2,0,1:T(8,128)(2,1)}, bf16[16,1,4096]{2,0,1:T(8,128)(2,1)S(1)}, u32[]{:S(2)}, u32[]{:S(2)}) %collective-permute-start.1) | collective-permute-done | bytes 131104 | tf_op jit(solution)/shard_map/ppermute | solution.py:17
  25.0 1.1 fusion.30
  26.3 0.1 fusion.69
  26.4 0.1 fusion.67
  26.5 0.1 fusion.65
  26.8 0.1 fusion.60
  27.0 0.1 fusion.55
  27.1 0.1 fusion.53
  27.3 0.1 fusion.51
  27.8 0.1 fusion.41
  27.9 0.1 fusion.39
  28.0 0.1 fusion.37
  28.4 3.4 %convolution_bitcast_fusion = f32[256,4096]{0,1:T(8,128)} fusion(bf16[432,4096]{1,0:T(8,128)(2,1)S(1)} %fusion.32, bf16[432,256]{1,0:T(8,128)(2,1)S(1)} %bitcast.261), kind=kOutput, calls=%fused_computation | convolution fusion | flops 905969664 | bytes 7954432 | tf_op jit(solution)/shard_map/dot_general | solution.py:91
  31.8 5.7 %copy.15 = f32[256,4096]{1,0:T(8,128)} copy(f32[256,4096]{0,1:T(8,128)} %convolution_bitcast_fusion) | data formatting | bytes 8388608
  37.5 70.7 %reduce-scatter.4.cloned.1.call-done = f32[16,4096]{1,0:T(8,128)} async-done(((f32[256,4096]{1,0:T(8,128)}), f32[16,4096]{1,0:T(8,128)}) %reduce-scatter.4.cloned.1.call-update) | async-done | bytes 262160
  108.2 1.5 copy.16
  109.8 0.2 fusion.24
  110.0 0.3 copy.9
  110.4 4.4 %collective-permute-start.2 = (bf16[16,1,4096]{2,0,1:T(8,128)(2,1)S(1)}, bf16[16,1,4096]{2,0,1:T(8,128)(2,1)S(1)}, u32[]{:S(2)}, u32[]{:S(2)}) collective-permute-start(bf16[16,1,4096]{2,0,1:T(8,128)(2,1)S(1)} %copy.9), channel_id=1, source_target_pairs={{0,16},{16,32},{32,48},{48,64},{64,80},{80,96},{96,112},{112,128},... | collective-permute-start | bytes 393224 | tf_op jit(solution)/shard_map/ppermute | solution.py:16
  114.7 1.5 collective-permute-start.3
  116.2 0.5 collective-permute-done.2
  116.7 6.5 %collective-permute-done.3 = bf16[16,1,4096]{2,0,1:T(8,128)(2,1)S(1)} collective-permute-done((bf16[16,1,4096]{2,0,1:T(8,128)(2,1)S(1)}, bf16[16,1,4096]{2,0,1:T(8,128)(2,1)S(1)}, u32[]{:S(2)}, u32[]{:S(2)}) %collective-permute-start.3) | collective-permute-done | bytes 131104 | tf_op jit(solution)/shard_map/ppermute | solution.py:17
  123.2 0.8 pad_maximum_fusion
  124.0 1.0 slice_bitcast_fusion.27
  125.0 43.9 %all-gather.2.cloned.1.call-done = bf16[256,3,4096]{2,0,1:T(8,128)(2,1)} async-done(((bf16[16,3,4096]{2,0,1:T(8,128)(2,1)}), bf16[256,3,4096]{2,0,1:T(8,128)(2,1)}) %all-gather.2.cloned.1.call-update) | async-done | bytes 6291472 | tf_op jit(solution)/shard_map/all_gather | solution.py:106
  168.9 2.6 %fusion.11 = bf16[2304,4096]{1,0:T(8,128)(2,1)S(1)} fusion(pred[4096]{0:T(1024)(128)(4,1)S(1)} %fusion.76, bf16[256,3,4096]{2,0,1:T(8,128)(2,1)} %all-gather.2.cloned.1.call-done), kind=kLoop, calls=%fused_computation.25 | loop fusion | flops 1048575 | bytes 8392704
  171.5 0.8 copy-done.2
  172.3 0.9 bitcast_dynamic-update-slice_fusion.1
  173.2 1.2 fusion.10
  174.4 3.2 %fusion.9 = (bf16[2304,4096]{1,0:T(8,128)(2,1)S(1)}, bf16[2304,4096]{1,0:T(8,128)(2,1)}) fusion(bf16[2304,4096]{1,0:T(8,128)(2,1)S(1)} %fusion.10, pred[4096]{0:T(1024)(128)(4,1)S(1)} %fusion.76, bf16[256,3,4096]{2,0,1:T(8,128)(2,1)S(1)} %copy-done.2), kind=kLoop, calls=%fused_computation.20 | loop fusion | flops 2097151 | bytes 10489856
  177.6 2.4 fusion.3
  180.0 3.7 %fusion.8 = (bf16[2304,4096]{1,0:T(8,128)(2,1)S(1)}, bf16[2304,4096]{1,0:T(8,128)(2,1)}) fusion(bf16[2304,4096]{1,0:T(8,128)(2,1)S(1)} %get-tuple-element.22, pred[4096]{0:T(1024)(128)(4,1)S(1)} %fusion.75, bf16[256,3,4096]{2,0,1:T(8,128)(2,1)S(1)} %copy-done.2, bf16[2304,4096]{1,0:T(8,128)(2,1)} %get-tuple-element.23), kind=kLoop, calls=%fused_computation.18 | loop fusion | flops 2097152 | bytes 10489856
  183.7 6.5 %copy-done.3 = bf16[2304,4096]{1,0:T(8,128)(2,1)} copy-done((bf16[2304,4096]{1,0:T(8,128)(2,1)}, bf16[2304,4096]{1,0:T(8,128)(2,1)S(1)}, u32[]{:S(2)}) %copy-start.3) | copy-done | bytes 18874392
  190.1 4.0 %fusion.7 = (bf16[2304,4096]{1,0:T(8,128)(2,1)}, bf16[2304,4096]{1,0:T(8,128)(2,1)}, bf16[2304,4096]{1,0:T(8,128)(2,1)S(1)}) fusion(bf16[2304,4096]{1,0:T(8,128)(2,1)} %copy-done.3, pred[4096]{0:T(1024)(128)(4,1)S(1)} %fusion.76, bf16[256,3,4096]{2,0,1:T(8,128)(2,1)S(1)} %copy-done.2, bf16[2304,4096]{1,0:T(8,128)(2,1)} %get-tuple-element.12), kind=kLoop, calls=%fused_computation.16 | loop fusion | flops 3145727 | bytes 12587008
  194.1 3.2 %bitcast_dynamic-update-slice_fusion = (bf16[2304,4096]{1,0:T(8,128)(2,1)}, bf16[2304,4096]{1,0:T(8,128)(2,1)S(1)}, bf16[2304,4096]{1,0:T(8,128)(2,1)}) fusion(bf16[2304,4096]{1,0:T(8,128)(2,1)} %get-tuple-element.8, bf16[256,3,4096]{2,0,1:T(8,128)(2,1)S(1)} %copy-done.2, bf16[2304,4096]{1,0:T(8,128)(2,1)S(1)} %get-tuple-element.10, ...), kind=kLoop, calls=%fused_computation.14 | loop fusion | bytes 14680064
  197.3 4.9 %fusion.6 = (bf16[2304,4096]{1,0:T(8,128)(2,1)}, bf16[2304,4096]{1,0:T(8,128)(2,1)}, bf16[2304,4096]{1,0:T(8,128)(2,1)S(1)}) fusion(bf16[2304,4096]{1,0:T(8,128)(2,1)} %get-tuple-element.19, pred[4096]{0:T(1024)(128)(4,1)S(1)} %fusion.75, bf16[256,3,4096]{2,0,1:T(8,128)(2,1)S(1)} %copy-done.2, bf16[2304,4096]{1,0:T(8,128)(2,1)} %get-tuple-element.21, ...), kind=kLoop, calls=%fused_computation.13 | loop fusion | flops 3145728 | bytes 12587008 | tf_op jit(solution)/shard_map/concatenate | solution.py:44
  202.2 1.2 fusion.15
  203.4 0.2 fusion.4
  203.6 1.2 fusion.14
  204.8 3.9 %fusion.13 = (bf16[2304,4096]{1,0:T(8,128)(2,1)S(1)}, bf16[2304,4096]{1,0:T(8,128)(2,1)}) fusion(bf16[2304,4096]{1,0:T(8,128)(2,1)S(1)} %fusion.14, pred[4096]{0:T(1024)(128)(4,1)S(1)} %fusion.76, bf16[256,3,4096]{2,0,1:T(8,128)(2,1)S(1)} %copy-done.2, bf16[2304,4096]{1,0:T(8,128)(2,1)} %get-tuple-element.6), kind=kLoop, calls=%fused_computation.30 | loop fusion | flops 2097152 | bytes 10489856
  208.7 4.1 %bitcast_dynamic-update-slice_fusion.2 = (bf16[2304,4096]{1,0:T(8,128)(2,1)S(1)}, bf16[2304,4096]{1,0:T(8,128)(2,1)}) fusion(bf16[2304,4096]{1,0:T(8,128)(2,1)S(1)} %get-tuple-element.17, bf16[256,3,4096]{2,0,1:T(8,128)(2,1)S(1)} %copy-done.2, bf16[2304,4096]{1,0:T(8,128)(2,1)} %get-tuple-element.18), kind=kLoop, calls=%fused_computation.28 | loop fusion | bytes 10485760
  212.8 3.9 %fusion.12 = (bf16[2304,4096]{1,0:T(8,128)(2,1)S(1)}, bf16[2304,4096]{1,0:T(8,128)(2,1)}) fusion(bf16[2304,4096]{1,0:T(8,128)(2,1)S(1)} %get-tuple-element.24, pred[4096]{0:T(1024)(128)(4,1)S(1)} %fusion.75, bf16[256,3,4096]{2,0,1:T(8,128)(2,1)S(1)} %copy-done.2, bf16[2304,4096]{1,0:T(8,128)(2,1)} %get-tuple-element.25), kind=kLoop, calls=%fused_computation.27 | loop fusion | flops 2097152 | bytes 10489856 | tf_op jit(solution)/shard_map/concatenate | solution.py:44
  216.7 7.9 %fusion.78 = f32[4096,16]{0,1:T(8,128)S(1)} fusion(bf16[2304,16]{0,1:T(8,128)(2,1)S(1)} %bitcast.264, bf16[2304,4096]{1,0:T(8,128)(2,1)} %get-tuple-element.16), kind=kOutput, calls=%fused_computation.144 | convolution fusion | flops 301989888 | bytes 19210240 | tf_op jit(solution)/shard_map/dot_general | solution.py:57
  224.6 2.6 %convolution_add_fusion.1 = f32[4096,16]{0,1:T(8,128)S(1)} fusion(f32[4096,16]{0,1:T(8,128)S(1)} %fusion.78, bf16[2304,16]{0,1:T(8,128)(2,1)S(1)} %bitcast.263, bf16[2304,4096]{1,0:T(8,128)(2,1)S(1)} %get-tuple-element.15), kind=kOutput, calls=%fused_computation.3 | convolution fusion | flops 302055424 | bytes 19472384 | tf_op jit(solution)/shard_map/dot_general | solution.py:57
  227.2 9.6 %fusion.2 = bf16[16,1,4096]{2,0,1:T(8,128)(2,1)} fusion(f32[4096,16]{0,1:T(8,128)S(1)} %convolution_add_fusion.1, bf16[2304,16]{0,1:T(8,128)(2,1)S(1)} %bitcast.262, bf16[2304,4096]{1,0:T(8,128)(2,1)} %get-tuple-element.5, f32[16]{0:T(128)S(1)} %copy-done.5), kind=kOutput, calls=%fused_computation.5 | convolution fusion | flops 302186496 | bytes 19341376 | tf_op jit(solution)/shard_map/dot_general | solution.py:57
  (38 shorter events, 1.2 us)
Async XLA Ops:
  6.5 21.9 %copy-start = (bf16[27,16,256]{2,1,0:T(8,128)(2,1)S(1)}, bf16[27,16,256]{2,1,0:T(8,128)(2,1)}, u32[]{:S(2)}) copy-start(bf16[27,16,256]{2,1,0:T(8,128)(2,1)} %param.6) | copy-start | bytes 663556
  6.5 20.7 %copy-start.4 = (bf16[16,1,4096]{2,0,1:T(8,128)(2,1)S(1)}, bf16[16,1,4096]{2,0,1:T(8,128)(2,1)}, u32[]{:S(2)}) copy-start(bf16[16,1,4096]{2,0,1:T(8,128)(2,1)} %param.5) | copy-start | bytes 393220
  6.5 101.7 %reduce-scatter.4.cloned.1.call-start = ((), (), s32[]{:S(2)}) async-start(), calls=%async_computation.2 | async-start | bytes 4456448
  6.5 8.3 %collective-permute-start = (bf16[16,1,4096]{2,0,1:T(8,128)(2,1)}, bf16[16,1,4096]{2,0,1:T(8,128)(2,1)S(1)}, u32[]{:S(2)}, u32[]{:S(2)}) collective-permute-start(bf16[16,1,4096]{2,0,1:T(8,128)(2,1)} %param.5), channel_id=1, source_target_pairs={{0,16},{16,32},{32,48},{48,64},{64,80},{80,96},{96,112},{112,128},... | collective-permute-start | bytes 393224 | tf_op jit(solution)/shard_map/ppermute | solution.py:16
  12.4 12.6 %collective-permute-start.1 = (bf16[16,1,4096]{2,0,1:T(8,128)(2,1)}, bf16[16,1,4096]{2,0,1:T(8,128)(2,1)S(1)}, u32[]{:S(2)}, u32[]{:S(2)}) collective-permute-start(bf16[16,1,4096]{2,0,1:T(8,128)(2,1)} %param.5), channel_id=1, source_target_pairs={{16,0},{32,16},{48,32},{64,48},{80,64},{96,80},{112,96},{128,112},... | collective-permute-start | bytes 393224 | tf_op jit(solution)/shard_map/ppermute | solution.py:17
  37.5 72.3 %copy-start.6 = (f32[16]{0:T(128)S(1)}, f32[16]{0:T(128)}, u32[]{:S(2)}) copy-start(f32[16]{0:T(128)} %param.7) | copy-start | bytes 196
  37.5 131.4 %all-gather.2.cloned.1.call-start = ((), (), s32[]{:S(2)}) async-start(), calls=%async_computation.1 | async-start | bytes 6684672 | tf_op jit(solution)/shard_map/all_gather | solution.py:106
  110.4 6.3 %collective-permute-start.2 = (bf16[16,1,4096]{2,0,1:T(8,128)(2,1)S(1)}, bf16[16,1,4096]{2,0,1:T(8,128)(2,1)S(1)}, u32[]{:S(2)}, u32[]{:S(2)}) collective-permute-start(bf16[16,1,4096]{2,0,1:T(8,128)(2,1)S(1)} %copy.9), channel_id=1, source_target_pairs={{0,16},{16,32},{32,48},{48,64},{64,80},{80,96},{96,112},{112,128},... | collective-permute-start | bytes 393224 | tf_op jit(solution)/shard_map/ppermute | solution.py:16
  114.7 8.5 %collective-permute-start.3 = (bf16[16,1,4096]{2,0,1:T(8,128)(2,1)S(1)}, bf16[16,1,4096]{2,0,1:T(8,128)(2,1)S(1)}, u32[]{:S(2)}, u32[]{:S(2)}) collective-permute-start(bf16[16,1,4096]{2,0,1:T(8,128)(2,1)S(1)} %copy.9), channel_id=1, source_target_pairs={{16,0},{32,16},{48,32},{64,48},{80,64},{96,80},{112,96},{128,112},... | collective-permute-start | bytes 393224 | tf_op jit(solution)/shard_map/ppermute | solution.py:17
  168.9 3.4 %copy-start.2 = (bf16[256,3,4096]{2,0,1:T(8,128)(2,1)S(1)}, bf16[256,3,4096]{2,0,1:T(8,128)(2,1)}, u32[]{:S(2)}) copy-start(bf16[256,3,4096]{2,0,1:T(8,128)(2,1)} %all-gather.2.cloned.1.call-done) | copy-start | bytes 18874372
  183.7 6.5 %copy-start.3 = (bf16[2304,4096]{1,0:T(8,128)(2,1)}, bf16[2304,4096]{1,0:T(8,128)(2,1)S(1)}, u32[]{:S(2)}) copy-start(bf16[2304,4096]{1,0:T(8,128)(2,1)S(1)} %get-tuple-element.11) | copy-start | bytes 56623108
  224.6 2.6 %copy-start.5 = (f32[16]{0:T(128)S(1)}, f32[16]{0:T(128)}, u32[]{:S(2)}) copy-start(f32[16]{0:T(128)} %param.9) | copy-start | bytes 196
  227.2 9.7 %copy-start.1 = (bf16[27,16,256]{2,1,0:T(8,128)(2,1)S(1)}, bf16[27,16,256]{2,1,0:T(8,128)(2,1)}, u32[]{:S(2)}) copy-start(bf16[27,16,256]{2,1,0:T(8,128)(2,1)} %param.6) | copy-start | bytes 663556
Sparse Core Ops, SparseCore 0:
  37.6 70.5 reduce-scatter.3
  124.1 44.7 all-gather.1
where the time goes:
time: 244 us
  waiting for transfers between devices  133 us (55%)
  other arithmetic  33.3 us (14%)
  local copies, waits for them, and re-layouts  27.3 us (11%)
  matrix products  23.5 us (10%)
  between operations  13.8 us (6%)
  starting transfers between devices  13 us (5%)
    unnamed x3, waiting for transfers between devices  70.7 us
    all_gather x1, waiting for transfers between devices, body(): lax.all_gather(hidden_rim, 'chan', axis=0, tiled=True)  43.9 us
    unnamed x31, local copies, waits for them, and re-layouts  26.9 us
    unnamed x25, other arithmetic  22.2 us
    dot_general x3, matrix products, fold_planes(): lax.dot_general(grouped[depth_tap], window, (((0,), (0,)), ((), ())), pre...  20.1 us
    ppermute x2, waiting for transfers between devices, extended(): after = lax.ppermute(leading, axis, down)  16.7 us
    ppermute x2, starting transfers between devices, extended(): before = lax.ppermute(last, axis, up)  10.2 us
    concatenate x2, other arithmetic, nine_taps(): per_plane.append(jnp.concatenate(windows, 0))  8.84 us
  transfers between devices with their start and end apart: 6, of which 6 were waited for; matrix products, arithmetic and copies ran while one was open for 0% of the time, Pallas kernels for 0%

commit v1 on v0

--- a/solution.py
+++ b/solution.py
@@ -103,7 +103,11 @@
     hidden = hidden.reshape(chan_local, slab_depth, cell_count)
     hidden_rim = extended(hidden, (("depth", 1),), 1)
     second_sum = fold_planes(
-        w_second, empty_sum, lax.all_gather(hidden_rim, "chan", axis=0, tiled=True)
+        w_second,
+        empty_sum,
+        jnp.concatenate(
+            lax.all_to_all(jnp.stack([hidden_rim] * lax.axis_size("chan")), "chan", 0, 0), axis=0
+        ),
     )
     block_out = (second_sum + b_second[:, None]).astype(jnp.bfloat16)
     return block_out.reshape(chan_local, slab_depth, cell_count)

time: 244 us -> 294 us (1.20)
  waiting for transfers between devices: 133 us -> 161 us
  starting transfers between devices: 13 us -> 19.6 us
  other arithmetic: 33.3 us -> 39.7 us
  matrix products: 23.5 us -> 28.4 us
    all_to_all x0 -> x1, waiting for transfers between devices: none -> 72 us  [body(): lax.all_to_all(jnp.stack([hidden_rim] * lax.axis_size('chan')), 'chan', 0...]
    all_gather x1 -> x0, waiting for transfers between devices: 43.9 us -> none  [body(): lax.all_gather(hidden_rim, 'chan', axis=0, tiled=True)]
    all_to_all x0 -> x1, starting transfers between devices: none -> 6.95 us  [body(): lax.all_to_all(jnp.stack([hidden_rim] * lax.axis_size('chan')), 'chan', 0...]
    unnamed x25, other arithmetic: 22.2 us -> 28.4 us
    dot_general x3, matrix products: 20.1 us -> 25 us  [fold_planes(): lax.dot_general(grouped[depth_tap], window, (((0,), (0,)), ((), ())), pre...]
    unnamed x31 -> x29, local copies, waits for them, and re-layouts: 26.9 us -> 23.2 us
    another operation x0 -> x1, local copies, waits for them, and re-layouts: none -> 3.38 us  [body(): jnp.stack([hidden_rim] * lax.axis_size('chan'))]
    all_to_all x0 -> x1, local copies, waits for them, and re-layouts: none -> 3.21 us  [body(): lax.all_to_all(jnp.stack([hidden_rim] * lax.axis_size('chan')), 'chan', 0...]
where the time goes in v1:
time: 294 us; the launch traced here: 293 us
  waiting for transfers between devices  161 us (55%)
  other arithmetic  39.7 us (14%)
  local copies, waits for them, and re-layouts  30.1 us (10%)
  matrix products  28.4 us (10%)
  starting transfers between devices  19.6 us (7%)
  between operations  13.7 us (5%)
    all_to_all x1, waiting for transfers between devices, body(): lax.all_to_all(jnp.stack([hidden_rim] * lax.axis_size('chan')), 'chan', 0...  72 us
    unnamed x2, waiting for transfers between devices  70.9 us
    unnamed x25, other arithmetic  28.4 us
    dot_general x3, matrix products, fold_planes(): lax.dot_general(grouped[depth_tap], window, (((0,), (0,)), ((), ())), pre...  25 us
    unnamed x29, local copies, waits for them, and re-layouts  23.2 us
    ppermute x2, waiting for transfers between devices, extended(): after = lax.ppermute(leading, axis, down)  16.8 us
    ppermute x2, starting transfers between devices, extended(): before = lax.ppermute(last, axis, up)  10 us
    concatenate x2, other arithmetic, nine_taps(): per_plane.append(jnp.concatenate(windows, 0))  9.88 us
  transfers between devices with their start and end apart: 6, of which 6 were waited for; matrix products, arithmetic and copies ran while one was open for 0% of the time, Pallas kernels for 0%

profile of v1, /device:TPU:1, one launch (start us, length us, event | category | flops | bytes accessed | tf_op | source)
XLA Modules:
  0.0 293.0 jit_solution(5695402608645757321)
XLA Ops:
  6.5 5.8 %collective-permute-start = (bf16[16,1,4096]{2,0,1:T(8,128)(2,1)}, bf16[16,1,4096]{2,0,1:T(8,128)(2,1)S(1)}, u32[]{:S(2)}, u32[]{:S(2)}) collective-permute-start(bf16[16,1,4096]{2,0,1:T(8,128)(2,1)} %param.5), channel_id=1, source_target_pairs={{0,16},{16,32},{32,48},{48,64},{64,80},{80,96},{96,112},{112,128},... | collective-permute-start | bytes 393224 | tf_op jit(solution)/shard_map/ppermute | solution.py:16
  12.4 1.3 collective-permute-start.1
  13.7 1.1 collective-permute-done
  14.9 10.2 %collective-permute-done.1 = bf16[16,1,4096]{2,0,1:T(8,128)(2,1)S(1)} collective-permute-done((bf16[16,1,4096]{2,0,1:T(8,128)(2,1)}, bf16[16,1,4096]{2,0,1:T(8,128)(2,1)S(1)}, u32[]{:S(2)}, u32[]{:S(2)}) %collective-permute-start.1) | collective-permute-done | bytes 131104 | tf_op jit(solution)/shard_map/ppermute | solution.py:17
  25.0 1.1 fusion.30
  26.3 0.1 fusion.69
  26.4 0.1 fusion.67
  26.5 0.1 fusion.65
  26.8 0.1 fusion.60
  27.0 0.1 fusion.55
  27.1 0.1 fusion.53
  27.3 0.1 fusion.51
  27.5 0.1 fusion.46
  27.8 0.1 fusion.41
  27.9 0.1 fusion.39
  28.0 0.1 fusion.37
  28.4 3.4 %convolution_bitcast_fusion = f32[256,4096]{0,1:T(8,128)} fusion(bf16[432,4096]{1,0:T(8,128)(2,1)S(1)} %fusion.32, bf16[432,256]{1,0:T(8,128)(2,1)S(1)} %bitcast.262), kind=kOutput, calls=%fused_computation | convolution fusion | flops 905969664 | bytes 7954432 | tf_op jit(solution)/shard_map/dot_general | solution.py:91
  31.8 5.7 %copy.24 = f32[256,4096]{1,0:T(8,128)} copy(f32[256,4096]{0,1:T(8,128)} %convolution_bitcast_fusion) | data formatting | bytes 8388608
  37.5 70.9 %reduce-scatter.4.cloned.1.call-done = f32[16,4096]{1,0:T(8,128)} async-done(((f32[256,4096]{1,0:T(8,128)}), f32[16,4096]{1,0:T(8,128)}) %reduce-scatter.4.cloned.1.call-update) | async-done | bytes 262160
  108.4 1.5 copy.25
  109.9 0.2 fusion.24
  110.1 0.3 copy.17
  110.5 4.2 %collective-permute-start.2 = (bf16[16,1,4096]{2,0,1:T(8,128)(2,1)S(1)}, bf16[16,1,4096]{2,0,1:T(8,128)(2,1)S(1)}, u32[]{:S(2)}, u32[]{:S(2)}) collective-permute-start(bf16[16,1,4096]{2,0,1:T(8,128)(2,1)S(1)} %copy.17), channel_id=1, source_target_pairs={{0,16},{16,32},{32,48},{48,64},{64,80},{80,96},{96,112},{112,128},... | collective-permute-start | bytes 393224 | tf_op jit(solution)/shard_map/ppermute | solution.py:16
  114.7 1.3 collective-permute-start.3
  116.0 0.6 collective-permute-done.2
  116.6 6.7 %collective-permute-done.3 = bf16[16,1,4096]{2,0,1:T(8,128)(2,1)S(1)} collective-permute-done((bf16[16,1,4096]{2,0,1:T(8,128)(2,1)S(1)}, bf16[16,1,4096]{2,0,1:T(8,128)(2,1)S(1)}, u32[]{:S(2)}, u32[]{:S(2)}) %collective-permute-start.3) | collective-permute-done | bytes 131104 | tf_op jit(solution)/shard_map/ppermute | solution.py:17
  123.3 3.4 %stack.2 = bf16[16,16,3,4096]{3,1,2,0:T(8,128)(2,1)} broadcast(bf16[16,3,4096]{2,0,1:T(8,128)(2,1)S(1)} %pad_maximum_fusion), dimensions={1,2,3} | broadcast | bytes 6684672 | tf_op jit(solution)/shard_map/stack | solution.py:109
  126.7 6.9 %all-to-all-start = ((bf16[16,16,3,4096]{3,1,2,0:T(8,128)(2,1)}), bf16[16,16,3,4096]{3,1,2,0:T(8,128)(2,1)}, u32[]{:S(2)}, u32[]{:S(2)}) async-start(bf16[16,16,3,4096]{3,1,2,0:T(8,128)(2,1)} %stack.2), calls=%async_computation | async-start | bytes 12582912 | tf_op jit(solution)/shard_map/all_to_all | solution.py:109
  133.7 72.0 %all-to-all-done = bf16[16,16,3,4096]{3,1,2,0:T(8,128)(2,1)} async-done(((bf16[16,16,3,4096]{3,1,2,0:T(8,128)(2,1)}), bf16[16,16,3,4096]{3,1,2,0:T(8,128)(2,1)}, u32[]{:S(2)}, u32[]{:S(2)}) %all-to-all-start) | async-done | bytes 6291488 | tf_op jit(solution)/shard_map/all_to_all | solution.py:109
  205.7 3.2 %copy.20 = bf16[16,16,3,4096]{3,1,0,2:T(8,128)(2,1)S(1)} copy(bf16[16,16,3,4096]{3,1,2,0:T(8,128)(2,1)} %all-to-all-done) | data formatting | bytes 12582912 | tf_op jit(solution)/shard_map/all_to_all | solution.py:109
  208.9 2.2 fusion.11
  211.2 2.3 bitcast_dynamic-update-slice_fusion.1
  213.5 2.6 fusion.10
  216.0 3.9 %fusion.9 = (bf16[2304,4096]{1,0:T(8,128)(2,1)}, bf16[2304,4096]{1,0:T(8,128)(2,1)}) fusion(bf16[2304,4096]{1,0:T(8,128)(2,1)} %fusion.10, pred[4096]{0:T(1024)(128)(4,1)S(1)} %fusion.76, bf16[256,3,4096]{2,0,1:T(8,128)(2,1)S(1)} %bitcast.266), kind=kLoop, calls=%fused_computation.20 | loop fusion | flops 2097151 | bytes 10489856
  219.9 3.1 %fusion.3 = (bf16[2304,4096]{1,0:T(8,128)(2,1)}, bf16[2304,4096]{1,0:T(8,128)(2,1)}) fusion(bf16[2304,4096]{1,0:T(8,128)(2,1)} %get-tuple-element.13, bf16[256,3,4096]{2,0,1:T(8,128)(2,1)S(1)} %bitcast.267, bf16[2304,4096]{1,0:T(8,128)(2,1)} %get-tuple-element.14), kind=kLoop, calls=%fused_computation.7 | loop fusion | bytes 12582912
  223.0 4.3 %fusion.8 = (bf16[2304,4096]{1,0:T(8,128)(2,1)}, bf16[2304,4096]{1,0:T(8,128)(2,1)}) fusion(bf16[2304,4096]{1,0:T(8,128)(2,1)} %get-tuple-element.22, pred[4096]{0:T(1024)(128)(4,1)S(1)} %fusion.75, bf16[256,3,4096]{2,0,1:T(8,128)(2,1)S(1)} %bitcast.268, bf16[2304,4096]{1,0:T(8,128)(2,1)} %get-tuple-element.23), kind=kLoop, calls=%fused_computation.18 | loop fusion | flops 2097152 | bytes 10489856
  227.3 4.4 %fusion.7 = (bf16[2304,4096]{1,0:T(8,128)(2,1)}, bf16[2304,4096]{1,0:T(8,128)(2,1)}, bf16[2304,4096]{1,0:T(8,128)(2,1)}) fusion(bf16[2304,4096]{1,0:T(8,128)(2,1)} %get-tuple-element.11, pred[4096]{0:T(1024)(128)(4,1)S(1)} %fusion.76, bf16[256,3,4096]{2,0,1:T(8,128)(2,1)S(1)} %bitcast.269, bf16[2304,4096]{1,0:T(8,128)(2,1)} %get-tuple-element.12), kind=kLoop, calls=%fused_computation.16 | loop fusion | flops 3145727 | bytes 12587008
  231.8 3.6 %bitcast_dynamic-update-slice_fusion = (bf16[2304,4096]{1,0:T(8,128)(2,1)}, bf16[2304,4096]{1,0:T(8,128)(2,1)}, bf16[2304,4096]{1,0:T(8,128)(2,1)}) fusion(bf16[2304,4096]{1,0:T(8,128)(2,1)} %get-tuple-element.8, bf16[256,3,4096]{2,0,1:T(8,128)(2,1)S(1)} %bitcast.270, bf16[2304,4096]{1,0:T(8,128)(2,1)} %get-tuple-element.10, ...), kind=kLoop, calls=%fused_computation.14 | loop fusion | bytes 14680064
  235.4 5.3 %fusion.6 = (bf16[2304,4096]{1,0:T(8,128)(2,1)}, bf16[2304,4096]{1,0:T(8,128)(2,1)}, bf16[2304,4096]{1,0:T(8,128)(2,1)}) fusion(bf16[2304,4096]{1,0:T(8,128)(2,1)} %get-tuple-element.19, pred[4096]{0:T(1024)(128)(4,1)S(1)} %fusion.75, bf16[256,3,4096]{2,0,1:T(8,128)(2,1)S(1)} %bitcast.271, bf16[2304,4096]{1,0:T(8,128)(2,1)} %get-tuple-element.21, ...), kind=kLoop, calls=%fused_computation.13 | loop fusion | flops 3145728 | bytes 12587008 | tf_op jit(solution)/shard_map/concatenate | solution.py:44
  240.6 2.6 fusion.15
  243.2 1.5 fusion.4
  244.7 2.5 fusion.14
  247.2 4.5 %fusion.13 = (bf16[2304,4096]{1,0:T(8,128)(2,1)}, bf16[2304,4096]{1,0:T(8,128)(2,1)}) fusion(bf16[2304,4096]{1,0:T(8,128)(2,1)} %fusion.14, pred[4096]{0:T(1024)(128)(4,1)S(1)} %fusion.76, bf16[256,3,4096]{2,0,1:T(8,128)(2,1)S(1)} %bitcast.275, bf16[2304,4096]{1,0:T(8,128)(2,1)} %get-tuple-element.6), kind=kLoop, calls=%fused_computation.30 | loop fusion | flops 2097152 | bytes 10489856
  251.7 4.8 %bitcast_dynamic-update-slice_fusion.2 = (bf16[2304,4096]{1,0:T(8,128)(2,1)}, bf16[2304,4096]{1,0:T(8,128)(2,1)}) fusion(bf16[2304,4096]{1,0:T(8,128)(2,1)} %get-tuple-element.17, bf16[256,3,4096]{2,0,1:T(8,128)(2,1)S(1)} %bitcast.276, bf16[2304,4096]{1,0:T(8,128)(2,1)} %get-tuple-element.18), kind=kLoop, calls=%fused_computation.28 | loop fusion | bytes 10485760
  256.5 4.6 %fusion.12 = (bf16[2304,4096]{1,0:T(8,128)(2,1)}, bf16[2304,4096]{1,0:T(8,128)(2,1)}) fusion(bf16[2304,4096]{1,0:T(8,128)(2,1)} %get-tuple-element.24, pred[4096]{0:T(1024)(128)(4,1)S(1)} %fusion.75, bf16[256,3,4096]{2,0,1:T(8,128)(2,1)S(1)} %bitcast.277, bf16[2304,4096]{1,0:T(8,128)(2,1)} %get-tuple-element.25), kind=kLoop, calls=%fused_computation.27 | loop fusion | flops 2097152 | bytes 10489856 | tf_op jit(solution)/shard_map/concatenate | solution.py:44
  261.1 7.7 %fusion.78 = f32[4096,16]{0,1:T(8,128)S(1)} fusion(bf16[2304,16]{0,1:T(8,128)(2,1)S(1)} %bitcast.280, bf16[2304,4096]{1,0:T(8,128)(2,1)} %get-tuple-element.16), kind=kOutput, calls=%fused_computation.144 | convolution fusion | flops 301989888 | bytes 19210240 | tf_op jit(solution)/shard_map/dot_general | solution.py:57
  268.8 7.7 %convolution_add_fusion.1 = f32[4096,16]{0,1:T(8,128)S(1)} fusion(f32[4096,16]{0,1:T(8,128)S(1)} %fusion.78, bf16[2304,16]{0,1:T(8,128)(2,1)S(1)} %bitcast.279, bf16[2304,4096]{1,0:T(8,128)(2,1)} %get-tuple-element.15), kind=kOutput, calls=%fused_computation.3 | convolution fusion | flops 302055424 | bytes 19472384 | tf_op jit(solution)/shard_map/dot_general | solution.py:57
  276.5 9.6 %fusion.2 = bf16[16,1,4096]{2,0,1:T(8,128)(2,1)} fusion(f32[4096,16]{0,1:T(8,128)S(1)} %convolution_add_fusion.1, bf16[2304,16]{0,1:T(8,128)(2,1)S(1)} %bitcast.278, bf16[2304,4096]{1,0:T(8,128)(2,1)} %get-tuple-element.5, f32[16]{0:T(128)S(1)} %copy-done.4), kind=kOutput, calls=%fused_computation.5 | convolution fusion | flops 302186496 | bytes 19341376 | tf_op jit(solution)/shard_map/dot_general | solution.py:57
  (37 shorter events, 1.1 us)
Async XLA Ops:
  6.5 21.9 %copy-start = (bf16[27,16,256]{2,1,0:T(8,128)(2,1)S(1)}, bf16[27,16,256]{2,1,0:T(8,128)(2,1)}, u32[]{:S(2)}) copy-start(bf16[27,16,256]{2,1,0:T(8,128)(2,1)} %param.6) | copy-start | bytes 663556
  6.5 20.7 %copy-start.2 = (bf16[16,1,4096]{2,0,1:T(8,128)(2,1)S(1)}, bf16[16,1,4096]{2,0,1:T(8,128)(2,1)}, u32[]{:S(2)}) copy-start(bf16[16,1,4096]{2,0,1:T(8,128)(2,1)} %param.5) | copy-start | bytes 393220
  6.5 101.8 %reduce-scatter.4.cloned.1.call-start = ((), (), s32[]{:S(2)}) async-start(), calls=%async_computation.2 | async-start | bytes 4456448
  6.5 8.3 %collective-permute-start = (bf16[16,1,4096]{2,0,1:T(8,128)(2,1)}, bf16[16,1,4096]{2,0,1:T(8,128)(2,1)S(1)}, u32[]{:S(2)}, u32[]{:S(2)}) collective-permute-start(bf16[16,1,4096]{2,0,1:T(8,128)(2,1)} %param.5), channel_id=1, source_target_pairs={{0,16},{16,32},{32,48},{48,64},{64,80},{80,96},{96,112},{112,128},... | collective-permute-start | bytes 393224 | tf_op jit(solution)/shard_map/ppermute | solution.py:16
  12.4 12.6 %collective-permute-start.1 = (bf16[16,1,4096]{2,0,1:T(8,128)(2,1)}, bf16[16,1,4096]{2,0,1:T(8,128)(2,1)S(1)}, u32[]{:S(2)}, u32[]{:S(2)}) collective-permute-start(bf16[16,1,4096]{2,0,1:T(8,128)(2,1)} %param.5), channel_id=1, source_target_pairs={{16,0},{32,16},{48,32},{64,48},{80,64},{96,80},{112,96},{128,112},... | collective-permute-start | bytes 393224 | tf_op jit(solution)/shard_map/ppermute | solution.py:17
  37.5 72.4 %copy-start.5 = (f32[16]{0:T(128)S(1)}, f32[16]{0:T(128)}, u32[]{:S(2)}) copy-start(f32[16]{0:T(128)} %param.7) | copy-start | bytes 196
  110.5 6.1 %collective-permute-start.2 = (bf16[16,1,4096]{2,0,1:T(8,128)(2,1)S(1)}, bf16[16,1,4096]{2,0,1:T(8,128)(2,1)S(1)}, u32[]{:S(2)}, u32[]{:S(2)}) collective-permute-start(bf16[16,1,4096]{2,0,1:T(8,128)(2,1)S(1)} %copy.17), channel_id=1, source_target_pairs={{0,16},{16,32},{32,48},{48,64},{64,80},{80,96},{96,112},{112,128},... | collective-permute-start | bytes 393224 | tf_op jit(solution)/shard_map/ppermute | solution.py:16
  114.7 8.6 %collective-permute-start.3 = (bf16[16,1,4096]{2,0,1:T(8,128)(2,1)S(1)}, bf16[16,1,4096]{2,0,1:T(8,128)(2,1)S(1)}, u32[]{:S(2)}, u32[]{:S(2)}) collective-permute-start(bf16[16,1,4096]{2,0,1:T(8,128)(2,1)S(1)} %copy.17), channel_id=1, source_target_pairs={{16,0},{32,16},{48,32},{64,48},{80,64},{96,80},{112,96},{128,112},... | collective-permute-start | bytes 393224 | tf_op jit(solution)/shard_map/ppermute | solution.py:17
  126.7 7.0 %copy-start.3 = (bf16[27,256,16]{1,2,0:T(8,128)(2,1)S(1)}, bf16[27,256,16]{1,2,0:T(8,128)(2,1)}, u32[]{:S(2)}) copy-start(bf16[27,256,16]{1,2,0:T(8,128)(2,1)} %param.8) | copy-start | bytes 663556
  126.7 79.0 %all-to-all-start = ((bf16[16,16,3,4096]{3,1,2,0:T(8,128)(2,1)}), bf16[16,16,3,4096]{3,1,2,0:T(8,128)(2,1)}, u32[]{:S(2)}, u32[]{:S(2)}) async-start(bf16[16,16,3,4096]{3,1,2,0:T(8,128)(2,1)} %stack.2), calls=%async_computation | async-start | bytes 12582912 | tf_op jit(solution)/shard_map/all_to_all | solution.py:109
  268.8 7.7 %copy-start.4 = (f32[16]{0:T(128)S(1)}, f32[16]{0:T(128)}, u32[]{:S(2)}) copy-start(f32[16]{0:T(128)} %param.9) | copy-start | bytes 196
  276.5 9.6 %copy-start.1 = (bf16[27,16,256]{2,1,0:T(8,128)(2,1)S(1)}, bf16[27,16,256]{2,1,0:T(8,128)(2,1)}, u32[]{:S(2)}) copy-start(bf16[27,16,256]{2,1,0:T(8,128)(2,1)} %param.6) | copy-start | bytes 663556
Sparse Core Ops, SparseCore 0:
  37.6 70.6 reduce-scatter.3
